TPU v7x, 256 devices: a whole 4x4x8 slice. The times are simulated.
256 devices in a mesh: span: 8 (over y, x_hi), tm: 32 (over x_lo, z, core).
Axes of the slice: x: 4 (x_hi: 2, x_lo: 2; x = x_hi * 2 + x_lo), y: 4, z: 8, core: 2. Of those that a mesh axis runs over, the one named last changes fastest.
Arguments:
- launched: float32 [8, 2, 110, 8192], P(None, None, None, 'tm'), may hold values from -1.5 to 1.5
- coupling: float32 [8, 2, 2, 2, 110, 110], P('span'), may hold values from -2 to 2
- impulse: float32 [8, 2, 2, 2, 129], P('span'), may hold values from -1.5 to 1.5
- amplifier: float32 [8, 2, 110], P('span'), may hold values from 0.9 to 1.11
- nonlinear: float32 [8, 2, 2], P('span'), may hold values from 0.002 to 0.008
Outputs:
- monitored: float32 [8, 8, 2, 110, 8192], P('span', None, None, None, 'tm')
All inputs are finite; a program needn't handle non-finite values.
Results may differ from a plain program's by a relative error of at most 0.0004.
Values sent between devices are 32-bit elements; how exact they have to be, the bound alone decides.
No kernel may reach another device: no remote copies, remote signals or barrier semaphores. Data moves between devices by JAX's collectives and lax.ppermute only.
A program may use at most 64 MiB of HBM per device.

v0:
```python
import jax
import jax.numpy as jnp
from jax import lax
from jax.sharding import PartitionSpec as P


def band(values, width):
    padded = jnp.concatenate([values, jnp.zeros((width,), jnp.float32)])
    tiled = jnp.tile(padded, width)[: width * 2 * width]
    return tiled.reshape(width, 2 * width).T


def prepare(coupling_group, impulse_group):
    half_taps = (impulse_group.shape[-1] - 1) // 2
    width = 2 * half_taps

    def toeplitz(pair):
        real_band = band(pair[0], width)
        imag_band = band(pair[1], width)
        upper = jnp.concatenate([real_band, imag_band], axis=1)
        lower = jnp.concatenate([-imag_band, real_band], axis=1)
        return jnp.concatenate([upper, lower], axis=0)

    filters = jax.vmap(jax.vmap(toeplitz))(impulse_group)
    real_part = coupling_group[:, :, 0]
    imag_part = coupling_group[:, :, 1]
    upper = jnp.concatenate([real_part, -imag_part], axis=-1)
    lower = jnp.concatenate([imag_part, real_part], axis=-1)
    return (filters, jnp.concatenate([upper, lower], axis=-2))


def disperse(extended, matrix, half_taps):
    width = 2 * half_taps
    frames, _, channels, extent = extended.shape
    block_count = extent // width - 1
    blocks = extended.reshape(frames, 2, channels, block_count + 1, width)
    windows = jnp.concatenate([blocks[..., :-1, :], blocks[..., 1:, :]], axis=-1)
    stacked = jnp.concatenate([windows[:, 0], windows[:, 1]], axis=-1)
    product = jnp.einsum("fcbu,uv->fcbv", stacked, matrix, precision=lax.Precision.HIGHEST)
    real_part = product[..., :width].reshape(frames, channels, block_count * width)
    imag_part = product[..., width:].reshape(frames, channels, block_count * width)
    return jnp.stack([real_part, imag_part], axis=1)


def couple(signal, mixer, coefficient):
    frames, _, channels, extent = signal.shape
    flat = signal.reshape(frames, 2 * channels, extent)
    mixed = jnp.einsum("de,fel->fdl", mixer, flat, precision=lax.Precision.HIGHEST).reshape(
        frames, 2, channels, extent
    )
    power = jnp.sum(mixed * mixed, axis=(1, 2))
    phase = coefficient * power[:, None, :]
    cosine = jnp.cos(phase)
    sine = jnp.sin(phase)
    real_part = mixed[:, 0]
    imag_part = mixed[:, 1]
    return jnp.stack(
        [real_part * cosine - imag_part * sine, real_part * sine + imag_part * cosine], axis=1
    )


def neighbours(block, halo):
    count = lax.axis_size("tm")
    forward = [(i, i + 1) for i in range(count - 1)]
    backward = [(i + 1, i) for i in range(count - 1)]
    extent = block.shape[-1]
    low = lax.ppermute(lax.slice_in_dim(block, extent - halo, None, axis=3), "tm", forward)
    high = lax.ppermute(lax.slice_in_dim(block, 0, halo, axis=3), "tm", backward)
    return jnp.concatenate([low, block, high], axis=3)


def group_pass(signal, filters, mixers, amplifier_group, nonlinear_group, origin, length):
    span_count, step_count = nonlinear_group.shape
    half_taps = filters.shape[-1] // 4
    halo = span_count * step_count * half_taps
    extent = signal.shape[-1]
    signal = neighbours(signal, halo)
    offset = -halo
    for span_index in range(span_count):
        for step_index in range(step_count):
            signal = disperse(signal, filters[span_index, step_index], half_taps)
            offset = offset + half_taps
            where = origin + offset + jnp.arange(signal.shape[-1], dtype=jnp.int32)
            inside = ((where >= 0) & (where < length)).astype(jnp.float32)
            signal = signal * inside
            signal = couple(
                signal, mixers[span_index, step_index], nonlinear_group[span_index, step_index]
            )
        signal = signal * amplifier_group[span_index][None, None, :, None]
    assert signal.shape[-1] == extent
    return signal


def shards(launched, coupling, impulse, amplifier, nonlinear):
    sections = lax.axis_size("span")
    section_index = lax.axis_index("span")
    frames_count, _, _, extent = launched.shape
    per_section = frames_count // sections
    length = extent * lax.axis_size("tm")
    origin = lax.axis_index("tm") * extent
    coupling_all = lax.all_gather(coupling, "span", axis=0, tiled=True)
    impulse_all = lax.all_gather(impulse, "span", axis=0, tiled=True)
    amplifier_all = lax.all_gather(amplifier, "span", axis=0, tiled=True)
    nonlinear_all = lax.all_gather(nonlinear, "span", axis=0, tiled=True)
    signal = lax.dynamic_slice_in_dim(launched, section_index * per_section, per_section, 0)

    def advance(signal, params):
        coupling_group, impulse_group, amplifier_group, nonlinear_group = params
        filters, mixers = prepare(coupling_group, impulse_group)
        signal = group_pass(
            signal, filters, mixers, amplifier_group, nonlinear_group, origin, length
        )
        return (signal, signal)

    _, stacked = lax.scan(
        advance, signal, (coupling_all, impulse_all, amplifier_all, nonlinear_all)
    )
    return lax.all_to_all(stacked, "span", 0, 1, tiled=True)


def solution(mesh):
    placed = (
        P(None, None, None, "tm"),
        P("span", None, None, None, None, None),
        P("span", None, None, None, None),
        P("span", None, None),
        P("span", None, None),
    )
    return jax.shard_map(
        shards,
        mesh=mesh,
        in_specs=placed,
        out_specs=P("span", None, None, None, "tm"),
        check_vma=False,
    )
```

profile of v0, /device:TPU:2, one launch (start us, length us, event | category | flops | bytes accessed | tf_op | source)
XLA Modules:
  0.0 689.6 jit_solution(1994653478486105164)
XLA Ops:
  8.7 22.9 %all_gather.14 = f32[8,2,2]{2,1,0:T(2,128)S(1)} all-gather(f32[1,2,2]{2,1,0:T(2,128)} %param.11), channel_id=1, replica_groups=mesh['span'=8,'tm'=32] {'span'}, dimensions={0}, use_global_device_ids=true | all-gather | bytes 144 | tf_op jit(solution)/shard_map/all_gather | solution.py:104
  31.7 18.4 %all_gather.15 = f32[8,2,110]{2,1,0:T(2,128)S(1)} all-gather(f32[1,2,110]{2,1,0:T(2,128)} %param.10), channel_id=1, replica_groups=mesh['span'=8,'tm'=32] {'span'}, dimensions={0}, use_global_device_ids=true | all-gather | bytes 7920 | tf_op jit(solution)/shard_map/all_gather | solution.py:103
  50.1 37.0 %all_gather.12 = f32[8,2,2,2,129]{4,3,2,1,0:T(2,128)} all-gather(f32[1,2,2,2,129]{4,3,2,1,0:T(2,128)} %param.9), channel_id=1, replica_groups=mesh['span'=8,'tm'=32] {'span'}, dimensions={0}, use_global_device_ids=true | all-gather | bytes 37152 | tf_op jit(solution)/shard_map/all_gather | solution.py:102
  87.1 568.2 %while.13 = (s32[]{:T(128)}, f32[1,2,110,256]{3,2,1,0:T(8,128)}, f32[8,1,2,110,256]{4,2,3,1,0:T(2,128)}, f32[8,2,2,2,129]{4,3,2,1,0:T(2,128)}, s32[]{:T(128)}, /...) while((s32[]{:T(128)}, f32[1,2,110,256]{3,2,1,0:T(8,128)}, ...), condition=%wide.region_5.6_spmd, body=%wide.region_0.5_spmd.sunk | while | flops 3470978304 | bytes 83243504 | solution.py:115
  89.0 2.4 collective-permute-start.1
  106.0 2.7 maximum_maximum_fusion.4
  154.8 8.4 %collective-permute-start = (f32[1,2,110,256]{3,2,1,0:T(8,128)}, f32[1,2,110,256]{3,2,1,0:T(8,128)}, u32[]{:S(2)}, u32[]{:S(2)}) collective-permute-start(f32[1,2,110,256]{3,2,1,0:T(8,128)} %get-tuple-element.367), channel_id=1, source_target_pairs={{1,0},{2,1},{3,2},{4,3},{5,4},{6,5},{7,6},{8,7},{9,8},{10,9},{11,1... | collective-permute-start | bytes 675848 | tf_op jit(solution)/shard_map/while/body/eval_jaxpr/ppermute | solution.py:68
  179.8 2.7 maximum_maximum_fusion.4
  228.6 5.7 collective-permute-start
  250.9 2.7 maximum_maximum_fusion.4
  299.7 5.7 collective-permute-start
  322.0 2.7 maximum_maximum_fusion.4
  354.8 2.4 multiply_reduce_fusion.9
  370.8 5.7 collective-permute-start
  393.1 2.7 maximum_maximum_fusion.4
  441.9 5.7 collective-permute-start
  464.2 2.7 maximum_maximum_fusion.4
  497.1 2.4 multiply_reduce_fusion.9
  513.0 5.7 collective-permute-start
  535.3 2.7 maximum_maximum_fusion.4
  584.1 5.7 collective-permute-start
  606.4 2.7 maximum_maximum_fusion.4
  639.3 2.4 multiply_reduce_fusion.9
  655.2 26.3 %all_to_all.12 = f32[8,1,2,110,256]{4,2,3,1,0:T(2,128)S(1)} all-to-all(f32[8,1,2,110,256]{4,2,3,1,0:T(2,128)} %get-tuple-element.90), channel_id=1, replica_groups=mesh['span'=8,'tm'=32] {'span'}, dimensions={0} | all-to-all | bytes 3604480 | tf_op jit(solution)/shard_map/all_to_all | solution.py:118
  (902 shorter events, 494.0 us)
Async XLA Ops:
  6.5 80.5 %all-gather.2.cloned.1.call-start = ((), (), s32[]{:S(2)}) async-start(), calls=%async_computation.1 | async-start | bytes 4055040 | tf_op jit(solution)/shard_map/all_gather | solution.py:101
  87.1 22.0 %collective-permute-start = (f32[1,2,110,256]{3,2,1,0:T(8,128)}, f32[1,2,110,256]{3,2,1,0:T(8,128)}, u32[]{:S(2)}, u32[]{:S(2)}) collective-permute-start(f32[1,2,110,256]{3,2,1,0:T(8,128)} %get-tuple-element.367), channel_id=1, source_target_pairs={{1,0},{2,1},{3,2},{4,3},{5,4},{6,5},{7,6},{8,7},{9,8},{10,9},{11,1... | collective-permute-start | bytes 675848 | tf_op jit(solution)/shard_map/while/body/eval_jaxpr/ppermute | solution.py:68
  89.0 20.1 %collective-permute-start.1 = (f32[1,2,110,256]{3,2,1,0:T(8,128)}, f32[1,2,110,256]{3,2,1,0:T(8,128)}, u32[]{:S(2)}, u32[]{:S(2)}) collective-permute-start(f32[1,2,110,256]{3,2,1,0:T(8,128)} %get-tuple-element.367), channel_id=1, source_target_pairs={{0,1},{1,2},{2,3},{3,4},{4,5},{5,6},{6,7},{7,8},{8,9},{9,10},{10,1... | collective-permute-start | bytes 675848 | tf_op jit(solution)/shard_map/while/body/eval_jaxpr/ppermute | solution.py:67
  99.1 7.0 %copy-start.1 = (f32[2,2,256,128]{3,2,1,0:T(8,128)S(1)}, f32[2,2,256,128]{3,2,1,0:T(8,128)}, u32[]{:S(2)}) copy-start(f32[2,2,256,128]{3,2,1,0:T(8,128)} %bitcast_negate_fusion.2) | copy-start | bytes 1572868 | tf_op jit(solution)/shard_map/while
  154.8 27.9 %collective-permute-start = (f32[1,2,110,256]{3,2,1,0:T(8,128)}, f32[1,2,110,256]{3,2,1,0:T(8,128)}, u32[]{:S(2)}, u32[]{:S(2)}) collective-permute-start(f32[1,2,110,256]{3,2,1,0:T(8,128)} %get-tuple-element.367), channel_id=1, source_target_pairs={{1,0},{2,1},{3,2},{4,3},{5,4},{6,5},{7,6},{8,7},{9,8},{10,9},{11,1... | collective-permute-start | bytes 675848 | tf_op jit(solution)/shard_map/while/body/eval_jaxpr/ppermute | solution.py:68
  163.2 19.6 %collective-permute-start.1 = (f32[1,2,110,256]{3,2,1,0:T(8,128)}, f32[1,2,110,256]{3,2,1,0:T(8,128)}, u32[]{:S(2)}, u32[]{:S(2)}) collective-permute-start(f32[1,2,110,256]{3,2,1,0:T(8,128)} %get-tuple-element.367), channel_id=1, source_target_pairs={{0,1},{1,2},{2,3},{3,4},{4,5},{5,6},{6,7},{7,8},{8,9},{9,10},{10,1... | collective-permute-start | bytes 675848 | tf_op jit(solution)/shard_map/while/body/eval_jaxpr/ppermute | solution.py:67
  172.8 7.0 %copy-start.1 = (f32[2,2,256,128]{3,2,1,0:T(8,128)S(1)}, f32[2,2,256,128]{3,2,1,0:T(8,128)}, u32[]{:S(2)}) copy-start(f32[2,2,256,128]{3,2,1,0:T(8,128)} %bitcast_negate_fusion.2) | copy-start | bytes 1572868 | tf_op jit(solution)/shard_map/while
  228.6 25.3 %collective-permute-start = (f32[1,2,110,256]{3,2,1,0:T(8,128)}, f32[1,2,110,256]{3,2,1,0:T(8,128)}, u32[]{:S(2)}, u32[]{:S(2)}) collective-permute-start(f32[1,2,110,256]{3,2,1,0:T(8,128)} %get-tuple-element.367), channel_id=1, source_target_pairs={{1,0},{2,1},{3,2},{4,3},{5,4},{6,5},{7,6},{8,7},{9,8},{10,9},{11,1... | collective-permute-start | bytes 675848 | tf_op jit(solution)/shard_map/while/body/eval_jaxpr/ppermute | solution.py:68
  234.3 19.6 %collective-permute-start.1 = (f32[1,2,110,256]{3,2,1,0:T(8,128)}, f32[1,2,110,256]{3,2,1,0:T(8,128)}, u32[]{:S(2)}, u32[]{:S(2)}) collective-permute-start(f32[1,2,110,256]{3,2,1,0:T(8,128)} %get-tuple-element.367), channel_id=1, source_target_pairs={{0,1},{1,2},{2,3},{3,4},{4,5},{5,6},{6,7},{7,8},{8,9},{9,10},{10,1... | collective-permute-start | bytes 675848 | tf_op jit(solution)/shard_map/while/body/eval_jaxpr/ppermute | solution.py:67
  243.9 7.0 %copy-start.1 = (f32[2,2,256,128]{3,2,1,0:T(8,128)S(1)}, f32[2,2,256,128]{3,2,1,0:T(8,128)}, u32[]{:S(2)}) copy-start(f32[2,2,256,128]{3,2,1,0:T(8,128)} %bitcast_negate_fusion.2) | copy-start | bytes 1572868 | tf_op jit(solution)/shard_map/while
  299.7 25.3 %collective-permute-start = (f32[1,2,110,256]{3,2,1,0:T(8,128)}, f32[1,2,110,256]{3,2,1,0:T(8,128)}, u32[]{:S(2)}, u32[]{:S(2)}) collective-permute-start(f32[1,2,110,256]{3,2,1,0:T(8,128)} %get-tuple-element.367), channel_id=1, source_target_pairs={{1,0},{2,1},{3,2},{4,3},{5,4},{6,5},{7,6},{8,7},{9,8},{10,9},{11,1... | collective-permute-start | bytes 675848 | tf_op jit(solution)/shard_map/while/body/eval_jaxpr/ppermute | solution.py:68
  305.4 19.6 %collective-permute-start.1 = (f32[1,2,110,256]{3,2,1,0:T(8,128)}, f32[1,2,110,256]{3,2,1,0:T(8,128)}, u32[]{:S(2)}, u32[]{:S(2)}) collective-permute-start(f32[1,2,110,256]{3,2,1,0:T(8,128)} %get-tuple-element.367), channel_id=1, source_target_pairs={{0,1},{1,2},{2,3},{3,4},{4,5},{5,6},{6,7},{7,8},{8,9},{9,10},{10,1... | collective-permute-start | bytes 675848 | tf_op jit(solution)/shard_map/while/body/eval_jaxpr/ppermute | solution.py:67
  370.8 25.3 %collective-permute-start = (f32[1,2,110,256]{3,2,1,0:T(8,128)}, f32[1,2,110,256]{3,2,1,0:T(8,128)}, u32[]{:S(2)}, u32[]{:S(2)}) collective-permute-start(f32[1,2,110,256]{3,2,1,0:T(8,128)} %get-tuple-element.367), channel_id=1, source_target_pairs={{1,0},{2,1},{3,2},{4,3},{5,4},{6,5},{7,6},{8,7},{9,8},{10,9},{11,1... | collective-permute-start | bytes 675848 | tf_op jit(solution)/shard_map/while/body/eval_jaxpr/ppermute | solution.py:68
  376.5 19.6 %collective-permute-start.1 = (f32[1,2,110,256]{3,2,1,0:T(8,128)}, f32[1,2,110,256]{3,2,1,0:T(8,128)}, u32[]{:S(2)}, u32[]{:S(2)}) collective-permute-start(f32[1,2,110,256]{3,2,1,0:T(8,128)} %get-tuple-element.367), channel_id=1, source_target_pairs={{0,1},{1,2},{2,3},{3,4},{4,5},{5,6},{6,7},{7,8},{8,9},{9,10},{10,1... | collective-permute-start | bytes 675848 | tf_op jit(solution)/shard_map/while/body/eval_jaxpr/ppermute | solution.py:67
  386.1 7.0 %copy-start.1 = (f32[2,2,256,128]{3,2,1,0:T(8,128)S(1)}, f32[2,2,256,128]{3,2,1,0:T(8,128)}, u32[]{:S(2)}) copy-start(f32[2,2,256,128]{3,2,1,0:T(8,128)} %bitcast_negate_fusion.2) | copy-start | bytes 1572868 | tf_op jit(solution)/shard_map/while
  441.9 25.3 %collective-permute-start = (f32[1,2,110,256]{3,2,1,0:T(8,128)}, f32[1,2,110,256]{3,2,1,0:T(8,128)}, u32[]{:S(2)}, u32[]{:S(2)}) collective-permute-start(f32[1,2,110,256]{3,2,1,0:T(8,128)} %get-tuple-element.367), channel_id=1, source_target_pairs={{1,0},{2,1},{3,2},{4,3},{5,4},{6,5},{7,6},{8,7},{9,8},{10,9},{11,1... | collective-permute-start | bytes 675848 | tf_op jit(solution)/shard_map/while/body/eval_jaxpr/ppermute | solution.py:68
  447.6 19.6 %collective-permute-start.1 = (f32[1,2,110,256]{3,2,1,0:T(8,128)}, f32[1,2,110,256]{3,2,1,0:T(8,128)}, u32[]{:S(2)}, u32[]{:S(2)}) collective-permute-start(f32[1,2,110,256]{3,2,1,0:T(8,128)} %get-tuple-element.367), channel_id=1, source_target_pairs={{0,1},{1,2},{2,3},{3,4},{4,5},{5,6},{6,7},{7,8},{8,9},{9,10},{10,1... | collective-permute-start | bytes 675848 | tf_op jit(solution)/shard_map/while/body/eval_jaxpr/ppermute | solution.py:67
  457.2 7.0 %copy-start.1 = (f32[2,2,256,128]{3,2,1,0:T(8,128)S(1)}, f32[2,2,256,128]{3,2,1,0:T(8,128)}, u32[]{:S(2)}) copy-start(f32[2,2,256,128]{3,2,1,0:T(8,128)} %bitcast_negate_fusion.2) | copy-start | bytes 1572868 | tf_op jit(solution)/shard_map/while
  513.0 25.3 %collective-permute-start = (f32[1,2,110,256]{3,2,1,0:T(8,128)}, f32[1,2,110,256]{3,2,1,0:T(8,128)}, u32[]{:S(2)}, u32[]{:S(2)}) collective-permute-start(f32[1,2,110,256]{3,2,1,0:T(8,128)} %get-tuple-element.367), channel_id=1, source_target_pairs={{1,0},{2,1},{3,2},{4,3},{5,4},{6,5},{7,6},{8,7},{9,8},{10,9},{11,1... | collective-permute-start | bytes 675848 | tf_op jit(solution)/shard_map/while/body/eval_jaxpr/ppermute | solution.py:68
  518.8 19.6 %collective-permute-start.1 = (f32[1,2,110,256]{3,2,1,0:T(8,128)}, f32[1,2,110,256]{3,2,1,0:T(8,128)}, u32[]{:S(2)}, u32[]{:S(2)}) collective-permute-start(f32[1,2,110,256]{3,2,1,0:T(8,128)} %get-tuple-element.367), channel_id=1, source_target_pairs={{0,1},{1,2},{2,3},{3,4},{4,5},{5,6},{6,7},{7,8},{8,9},{9,10},{10,1... | collective-permute-start | bytes 675848 | tf_op jit(solution)/shard_map/while/body/eval_jaxpr/ppermute | solution.py:67
  528.3 7.0 %copy-start.1 = (f32[2,2,256,128]{3,2,1,0:T(8,128)S(1)}, f32[2,2,256,128]{3,2,1,0:T(8,128)}, u32[]{:S(2)}) copy-start(f32[2,2,256,128]{3,2,1,0:T(8,128)} %bitcast_negate_fusion.2) | copy-start | bytes 1572868 | tf_op jit(solution)/shard_map/while
  584.1 25.3 %collective-permute-start = (f32[1,2,110,256]{3,2,1,0:T(8,128)}, f32[1,2,110,256]{3,2,1,0:T(8,128)}, u32[]{:S(2)}, u32[]{:S(2)}) collective-permute-start(f32[1,2,110,256]{3,2,1,0:T(8,128)} %get-tuple-element.367), channel_id=1, source_target_pairs={{1,0},{2,1},{3,2},{4,3},{5,4},{6,5},{7,6},{8,7},{9,8},{10,9},{11,1... | collective-permute-start | bytes 675848 | tf_op jit(solution)/shard_map/while/body/eval_jaxpr/ppermute | solution.py:68
  589.9 19.6 %collective-permute-start.1 = (f32[1,2,110,256]{3,2,1,0:T(8,128)}, f32[1,2,110,256]{3,2,1,0:T(8,128)}, u32[]{:S(2)}, u32[]{:S(2)}) collective-permute-start(f32[1,2,110,256]{3,2,1,0:T(8,128)} %get-tuple-element.367), channel_id=1, source_target_pairs={{0,1},{1,2},{2,3},{3,4},{4,5},{5,6},{6,7},{7,8},{8,9},{9,10},{10,1... | collective-permute-start | bytes 675848 | tf_op jit(solution)/shard_map/while/body/eval_jaxpr/ppermute | solution.py:67
  599.4 7.0 %copy-start.1 = (f32[2,2,256,128]{3,2,1,0:T(8,128)S(1)}, f32[2,2,256,128]{3,2,1,0:T(8,128)}, u32[]{:S(2)}) copy-start(f32[2,2,256,128]{3,2,1,0:T(8,128)} %bitcast_negate_fusion.2) | copy-start | bytes 1572868 | tf_op jit(solution)/shard_map/while
  (26 other events, 88.5 us)
Sparse Core Ops, SparseCore 0:
  9.9 74.1 all-gather.1
where the time goes:
time: 698 us; the launch traced here: 690 us
  local copies, waits for them, and re-layouts  275 us (39%)
  other arithmetic  132 us (19%)
  blocking collectives  105 us (15%)
  matrix products  98.7 us (14%)
  starting transfers between devices  60.5 us (9%)
  between operations  13.4 us (2%)
    dot_general x32, matrix products, disperse(): jnp.einsum('fcbu,uv->fcbv', stacked, matrix, precision=lax.Precision.HIGH...  59.1 us
    ppermute x8, starting transfers between devices, neighbours(): lax.ppermute(lax.slice_in_dim(block, 0, halo, axis=3), 'tm', backward)  44.6 us
    reshape x32, local copies, waits for them, and re-layouts, band(): return tiled.reshape(width, 2 * width).T  40 us
    dot_general x32, matrix products, couple(): jnp.einsum('de,fel->fdl', mixer, flat, precision=lax.Precision.HIGHEST)  39.6 us
    all_gather x1, blocking collectives, shards(): impulse_all = lax.all_gather(impulse, 'span', axis=0, tiled=True)  37 us
    while x80, local copies, waits for them, and re-layouts  28.2 us
    all_to_all x1, blocking collectives, shards(): return lax.all_to_all(stacked, 'span', 0, 1, tiled=True)  26.3 us
    mul x32, other arithmetic, group_pass(): signal = signal * inside  26.3 us
  transfers between devices with their start and end apart: 17, of which 0 were waited for; matrix products, arithmetic and copies ran while one was open for 20% of the time, Pallas kernels for 0%

commit v1 on v0

--- a/solution.py
+++ b/solution.py
@@ -2,6 +2,12 @@
 import jax.numpy as jnp
 from jax import lax
 from jax.sharding import PartitionSpec as P
+
+
+def convert_node_in(point):
+    big = jnp.stack(lax.axis_size("span") * [point])
+    right_arr = jnp.concatenate(lax.all_to_all(big, "span", 0, 0), 0)
+    return right_arr
 
 
 def band(values, width):
@@ -99,7 +105,7 @@
     length = extent * lax.axis_size("tm")
     origin = lax.axis_index("tm") * extent
     coupling_all = lax.all_gather(coupling, "span", axis=0, tiled=True)
-    impulse_all = lax.all_gather(impulse, "span", axis=0, tiled=True)
+    impulse_all = convert_node_in(impulse)
     amplifier_all = lax.all_gather(amplifier, "span", axis=0, tiled=True)
     nonlinear_all = lax.all_gather(nonlinear, "span", axis=0, tiled=True)
     signal = lax.dynamic_slice_in_dim(launched, section_index * per_section, per_section, 0)

time: 698 us -> 664 us (0.951)
  blocking collectives: 105 us -> 68.5 us
  waiting for transfers between devices: 0.75 us -> 26.2 us
  local copies, waits for them, and re-layouts: 275 us -> 255 us
  other arithmetic: 132 us -> 124 us
    all_gather x1 -> x0, blocking collectives: 37 us -> none  [shards(): impulse_all = lax.all_gather(impulse, 'span', axis=0, tiled=True)]
    all_gather x1, waiting for transfers between devices: 0.01 us -> 25.4 us  [shards(): coupling_all = lax.all_gather(coupling, 'span', axis=0, tiled=True)]
    reshape x32, local copies, waits for them, and re-layouts: 40 us -> 25 us  [band(): return tiled.reshape(width, 2 * width).T]
    concatenate x8, other arithmetic: 21.3 us -> 12 us  [toeplitz(): return jnp.concatenate([upper, lower], axis=0)]
    dynamic_slice x40 -> x24, local copies, waits for them, and re-layouts: 14.3 us -> 8.73 us  [shards(): lax.scan(advance, signal, (coupling_all, impulse_all, amplifier_all, nonl...]
  transfers between devices with their start and end apart: 17 -> 18, of which waited for: 0 -> 1; matrix products, arithmetic and copies ran while one was open for 20% -> 17% of each run, Pallas kernels for 0% -> 0%
where the time goes in v1:
time: 664 us; the launch traced here: 656 us
  local copies, waits for them, and re-layouts  255 us (38%)
  other arithmetic  124 us (19%)
  matrix products  98.7 us (15%)
  blocking collectives  68.5 us (10%)
  starting transfers between devices  66.5 us (10%)
  waiting for transfers between devices  26.2 us (4%)
  between operations  13.4 us (2%)
    dot_general x32, matrix products, disperse(): jnp.einsum('fcbu,uv->fcbv', stacked, matrix, precision=lax.Precision.HIGH...  59.1 us
    ppermute x8, starting transfers between devices, neighbours(): lax.ppermute(lax.slice_in_dim(block, 0, halo, axis=3), 'tm', backward)  45.1 us
    dot_general x32, matrix products, couple(): jnp.einsum('de,fel->fdl', mixer, flat, precision=lax.Precision.HIGHEST)  39.7 us
    while x80, local copies, waits for them, and re-layouts  28.4 us
    mul x32, other arithmetic, group_pass(): signal = signal * inside  26.3 us
    all_to_all x1, blocking collectives, shards(): return lax.all_to_all(stacked, 'span', 0, 1, tiled=True)  26.1 us
    mul x48, local copies, waits for them, and re-layouts, group_pass(): signal = signal * inside  26 us
    all_gather x1, waiting for transfers between devices, shards(): coupling_all = lax.all_gather(coupling, 'span', axis=0, tiled=True)  25.4 us
  transfers between devices with their start and end apart: 18, of which 1 were waited for; matrix products, arithmetic and copies ran while one was open for 17% of the time, Pallas kernels for 0%

profile of v1, /device:TPU:2, one launch (start us, length us, event | category | flops | bytes accessed | tf_op | source)
XLA Modules:
  0.0 656.2 jit_solution(14613084394353494460)
XLA Ops:
  8.6 6.0 all-to-all-start
  15.4 24.0 %all_gather.10 = f32[8,2,2]{2,1,0:T(2,128)S(1)} all-gather(f32[1,2,2]{2,1,0:T(2,128)} %param.11), channel_id=1, replica_groups=mesh['span'=8,'tm'=32] {'span'}, dimensions={0}, use_global_device_ids=true | all-gather | bytes 144 | tf_op jit(solution)/shard_map/all_gather | solution.py:110
  39.4 18.4 %all_gather.11 = f32[8,2,110]{2,1,0:T(2,128)S(1)} all-gather(f32[1,2,110]{2,1,0:T(2,128)} %param.10), channel_id=1, replica_groups=mesh['span'=8,'tm'=32] {'span'}, dimensions={0}, use_global_device_ids=true | all-gather | bytes 7920 | tf_op jit(solution)/shard_map/all_gather | solution.py:109
  57.8 25.4 %all-gather.2.cloned.1.call-done = f32[8,2,2,2,110,110]{5,3,4,2,1,0:T(2,128)} async-done(((f32[1,2,2,2,110,110]{5,3,4,2,1,0:T(2,128)}), f32[8,2,2,2,110,110]{5,3,4,2,1,0:T(2,128)}) %all-gather.2.cloned.1.call-update) | async-done | bytes 3097616 | tf_op jit(solution)/shard_map/all_gather | solution.py:107
  83.3 538.8 %while.13 = (s32[]{:T(128)}, f32[1,2,110,256]{3,2,1,0:T(8,128)}, f32[8,1,2,110,256]{4,2,3,1,0:T(2,128)}, f32[8,2,2,2,129]{4,2,1,3,0:T(2,128)}, s32[]{:T(128)}, /...) while((s32[]{:T(128)}, f32[1,2,110,256]{3,2,1,0:T(8,128)}, ...), condition=%wide.region_5.6_spmd, body=%wide.region_0.5_spmd.sunk | while | flops 3470978304 | bytes 83235248 | solution.py:121
  83.3 4.8 collective-permute-start
  109.9 2.2 copy.115
  133.7 2.4 multiply_reduce_fusion.9
  149.8 5.7 collective-permute-start
  201.2 2.4 multiply_reduce_fusion.9
  217.3 5.8 collective-permute-start
  244.9 2.2 copy.115
  268.6 2.4 multiply_reduce_fusion.9
  284.8 5.7 collective-permute-start
  336.1 2.4 multiply_reduce_fusion.9
  352.2 5.8 collective-permute-start
  403.6 2.4 multiply_reduce_fusion.9
  419.7 5.7 collective-permute-start
  471.0 2.4 multiply_reduce_fusion.9
  487.1 5.8 collective-permute-start
  538.5 2.4 multiply_reduce_fusion.9
  554.6 5.7 collective-permute-start
  606.0 2.4 multiply_reduce_fusion.9
  622.1 26.1 %all_to_all.17 = f32[8,1,2,110,256]{4,2,3,1,0:T(2,128)S(1)} all-to-all(f32[8,1,2,110,256]{4,2,3,1,0:T(2,128)} %get-tuple-element.90), channel_id=1, replica_groups=mesh['span'=8,'tm'=32] {'span'}, dimensions={0} | all-to-all | bytes 3604480 | tf_op jit(solution)/shard_map/all_to_all | solution.py:124
  (897 shorter events, 469.8 us)
Async XLA Ops:
  6.5 8.1 %copy-start = (f32[8,2,110,256]{3,1,2,0:T(2,128)S(1)}, f32[8,2,110,256]{3,1,2,0:T(2,128)}, u32[]{:S(2)}) copy-start(f32[8,2,110,256]{3,1,2,0:T(2,128)} %param.7) | copy-start | bytes 5406724
  6.5 76.7 %all-gather.2.cloned.1.call-start = ((), (), s32[]{:S(2)}) async-start(), calls=%async_computation.2 | async-start | bytes 4055040 | tf_op jit(solution)/shard_map/all_gather | solution.py:107
  8.6 49.2 %all-to-all-start = ((f32[8,1,2,2,2,129]{5,3,2,4,1,0:T(2,128)}), f32[8,1,2,2,2,129]{5,3,2,4,1,0:T(2,128)}, u32[]{:S(2)}, u32[]{:S(2)}) async-start(f32[8,1,2,2,2,129]{5,3,2,4,1,0:T(2,128)} %stack.77), calls=%async_computation | async-start | bytes 131072 | tf_op jit(solution)/shard_map/all_to_all | solution.py:9
  83.3 20.6 %collective-permute-start = (f32[1,2,110,256]{3,2,1,0:T(8,128)}, f32[1,2,110,256]{3,2,1,0:T(8,128)}, u32[]{:S(2)}, u32[]{:S(2)}) collective-permute-start(f32[1,2,110,256]{3,2,1,0:T(8,128)} %get-tuple-element.367), channel_id=1, source_target_pairs={{1,0},{2,1},{3,2},{4,3},{5,4},{6,5},{7,6},{8,7},{9,8},{10,9},{11,1... | collective-permute-start | bytes 675848 | tf_op jit(solution)/shard_map/while/body/eval_jaxpr/ppermute | solution.py:74
  88.1 15.8 %collective-permute-start.1 = (f32[1,2,110,256]{3,2,1,0:T(8,128)}, f32[1,2,110,256]{3,2,1,0:T(8,128)}, u32[]{:S(2)}, u32[]{:S(2)}) collective-permute-start(f32[1,2,110,256]{3,2,1,0:T(8,128)} %get-tuple-element.367), channel_id=1, source_target_pairs={{0,1},{1,2},{2,3},{3,4},{4,5},{5,6},{6,7},{7,8},{8,9},{9,10},{10,1... | collective-permute-start | bytes 675848 | tf_op jit(solution)/shard_map/while/body/eval_jaxpr/ppermute | solution.py:73
  97.6 4.4 copy-start.1
  149.8 21.5 %collective-permute-start = (f32[1,2,110,256]{3,2,1,0:T(8,128)}, f32[1,2,110,256]{3,2,1,0:T(8,128)}, u32[]{:S(2)}, u32[]{:S(2)}) collective-permute-start(f32[1,2,110,256]{3,2,1,0:T(8,128)} %get-tuple-element.367), channel_id=1, source_target_pairs={{1,0},{2,1},{3,2},{4,3},{5,4},{6,5},{7,6},{8,7},{9,8},{10,9},{11,1... | collective-permute-start | bytes 675848 | tf_op jit(solution)/shard_map/while/body/eval_jaxpr/ppermute | solution.py:74
  155.6 15.8 %collective-permute-start.1 = (f32[1,2,110,256]{3,2,1,0:T(8,128)}, f32[1,2,110,256]{3,2,1,0:T(8,128)}, u32[]{:S(2)}, u32[]{:S(2)}) collective-permute-start(f32[1,2,110,256]{3,2,1,0:T(8,128)} %get-tuple-element.367), channel_id=1, source_target_pairs={{0,1},{1,2},{2,3},{3,4},{4,5},{5,6},{6,7},{7,8},{8,9},{9,10},{10,1... | collective-permute-start | bytes 675848 | tf_op jit(solution)/shard_map/while/body/eval_jaxpr/ppermute | solution.py:73
  165.1 4.4 copy-start.1
  217.3 21.5 %collective-permute-start = (f32[1,2,110,256]{3,2,1,0:T(8,128)}, f32[1,2,110,256]{3,2,1,0:T(8,128)}, u32[]{:S(2)}, u32[]{:S(2)}) collective-permute-start(f32[1,2,110,256]{3,2,1,0:T(8,128)} %get-tuple-element.367), channel_id=1, source_target_pairs={{1,0},{2,1},{3,2},{4,3},{5,4},{6,5},{7,6},{8,7},{9,8},{10,9},{11,1... | collective-permute-start | bytes 675848 | tf_op jit(solution)/shard_map/while/body/eval_jaxpr/ppermute | solution.py:74
  223.0 15.8 %collective-permute-start.1 = (f32[1,2,110,256]{3,2,1,0:T(8,128)}, f32[1,2,110,256]{3,2,1,0:T(8,128)}, u32[]{:S(2)}, u32[]{:S(2)}) collective-permute-start(f32[1,2,110,256]{3,2,1,0:T(8,128)} %get-tuple-element.367), channel_id=1, source_target_pairs={{0,1},{1,2},{2,3},{3,4},{4,5},{5,6},{6,7},{7,8},{8,9},{9,10},{10,1... | collective-permute-start | bytes 675848 | tf_op jit(solution)/shard_map/while/body/eval_jaxpr/ppermute | solution.py:73
  232.6 4.4 copy-start.1
  284.8 21.5 %collective-permute-start = (f32[1,2,110,256]{3,2,1,0:T(8,128)}, f32[1,2,110,256]{3,2,1,0:T(8,128)}, u32[]{:S(2)}, u32[]{:S(2)}) collective-permute-start(f32[1,2,110,256]{3,2,1,0:T(8,128)} %get-tuple-element.367), channel_id=1, source_target_pairs={{1,0},{2,1},{3,2},{4,3},{5,4},{6,5},{7,6},{8,7},{9,8},{10,9},{11,1... | collective-permute-start | bytes 675848 | tf_op jit(solution)/shard_map/while/body/eval_jaxpr/ppermute | solution.py:74
  290.5 15.8 %collective-permute-start.1 = (f32[1,2,110,256]{3,2,1,0:T(8,128)}, f32[1,2,110,256]{3,2,1,0:T(8,128)}, u32[]{:S(2)}, u32[]{:S(2)}) collective-permute-start(f32[1,2,110,256]{3,2,1,0:T(8,128)} %get-tuple-element.367), channel_id=1, source_target_pairs={{0,1},{1,2},{2,3},{3,4},{4,5},{5,6},{6,7},{7,8},{8,9},{9,10},{10,1... | collective-permute-start | bytes 675848 | tf_op jit(solution)/shard_map/while/body/eval_jaxpr/ppermute | solution.py:73
  352.2 21.5 %collective-permute-start = (f32[1,2,110,256]{3,2,1,0:T(8,128)}, f32[1,2,110,256]{3,2,1,0:T(8,128)}, u32[]{:S(2)}, u32[]{:S(2)}) collective-permute-start(f32[1,2,110,256]{3,2,1,0:T(8,128)} %get-tuple-element.367), channel_id=1, source_target_pairs={{1,0},{2,1},{3,2},{4,3},{5,4},{6,5},{7,6},{8,7},{9,8},{10,9},{11,1... | collective-permute-start | bytes 675848 | tf_op jit(solution)/shard_map/while/body/eval_jaxpr/ppermute | solution.py:74
  358.0 15.8 %collective-permute-start.1 = (f32[1,2,110,256]{3,2,1,0:T(8,128)}, f32[1,2,110,256]{3,2,1,0:T(8,128)}, u32[]{:S(2)}, u32[]{:S(2)}) collective-permute-start(f32[1,2,110,256]{3,2,1,0:T(8,128)} %get-tuple-element.367), channel_id=1, source_target_pairs={{0,1},{1,2},{2,3},{3,4},{4,5},{5,6},{6,7},{7,8},{8,9},{9,10},{10,1... | collective-permute-start | bytes 675848 | tf_op jit(solution)/shard_map/while/body/eval_jaxpr/ppermute | solution.py:73
  367.5 4.4 copy-start.1
  419.7 21.5 %collective-permute-start = (f32[1,2,110,256]{3,2,1,0:T(8,128)}, f32[1,2,110,256]{3,2,1,0:T(8,128)}, u32[]{:S(2)}, u32[]{:S(2)}) collective-permute-start(f32[1,2,110,256]{3,2,1,0:T(8,128)} %get-tuple-element.367), channel_id=1, source_target_pairs={{1,0},{2,1},{3,2},{4,3},{5,4},{6,5},{7,6},{8,7},{9,8},{10,9},{11,1... | collective-permute-start | bytes 675848 | tf_op jit(solution)/shard_map/while/body/eval_jaxpr/ppermute | solution.py:74
  425.4 15.8 %collective-permute-start.1 = (f32[1,2,110,256]{3,2,1,0:T(8,128)}, f32[1,2,110,256]{3,2,1,0:T(8,128)}, u32[]{:S(2)}, u32[]{:S(2)}) collective-permute-start(f32[1,2,110,256]{3,2,1,0:T(8,128)} %get-tuple-element.367), channel_id=1, source_target_pairs={{0,1},{1,2},{2,3},{3,4},{4,5},{5,6},{6,7},{7,8},{8,9},{9,10},{10,1... | collective-permute-start | bytes 675848 | tf_op jit(solution)/shard_map/while/body/eval_jaxpr/ppermute | solution.py:73
  434.9 4.4 copy-start.1
  487.1 21.5 %collective-permute-start = (f32[1,2,110,256]{3,2,1,0:T(8,128)}, f32[1,2,110,256]{3,2,1,0:T(8,128)}, u32[]{:S(2)}, u32[]{:S(2)}) collective-permute-start(f32[1,2,110,256]{3,2,1,0:T(8,128)} %get-tuple-element.367), channel_id=1, source_target_pairs={{1,0},{2,1},{3,2},{4,3},{5,4},{6,5},{7,6},{8,7},{9,8},{10,9},{11,1... | collective-permute-start | bytes 675848 | tf_op jit(solution)/shard_map/while/body/eval_jaxpr/ppermute | solution.py:74
  492.9 15.8 %collective-permute-start.1 = (f32[1,2,110,256]{3,2,1,0:T(8,128)}, f32[1,2,110,256]{3,2,1,0:T(8,128)}, u32[]{:S(2)}, u32[]{:S(2)}) collective-permute-start(f32[1,2,110,256]{3,2,1,0:T(8,128)} %get-tuple-element.367), channel_id=1, source_target_pairs={{0,1},{1,2},{2,3},{3,4},{4,5},{5,6},{6,7},{7,8},{8,9},{9,10},{10,1... | collective-permute-start | bytes 675848 | tf_op jit(solution)/shard_map/while/body/eval_jaxpr/ppermute | solution.py:73
  554.6 21.5 %collective-permute-start = (f32[1,2,110,256]{3,2,1,0:T(8,128)}, f32[1,2,110,256]{3,2,1,0:T(8,128)}, u32[]{:S(2)}, u32[]{:S(2)}) collective-permute-start(f32[1,2,110,256]{3,2,1,0:T(8,128)} %get-tuple-element.367), channel_id=1, source_target_pairs={{1,0},{2,1},{3,2},{4,3},{5,4},{6,5},{7,6},{8,7},{9,8},{10,9},{11,1... | collective-permute-start | bytes 675848 | tf_op jit(solution)/shard_map/while/body/eval_jaxpr/ppermute | solution.py:74
  560.4 15.8 %collective-permute-start.1 = (f32[1,2,110,256]{3,2,1,0:T(8,128)}, f32[1,2,110,256]{3,2,1,0:T(8,128)}, u32[]{:S(2)}, u32[]{:S(2)}) collective-permute-start(f32[1,2,110,256]{3,2,1,0:T(8,128)} %get-tuple-element.367), channel_id=1, source_target_pairs={{0,1},{1,2},{2,3},{3,4},{4,5},{5,6},{6,7},{7,8},{8,9},{9,10},{10,1... | collective-permute-start | bytes 675848 | tf_op jit(solution)/shard_map/while/body/eval_jaxpr/ppermute | solution.py:73
  (27 other events, 67.6 us)
Sparse Core Ops, SparseCore 0:
  9.9 73.2 all-gather.1
